TPU v7x, 512 devices: a whole 4x8x8 slice. The times are simulated.
512 devices in a mesh: row: 32 (over z, x), col: 16 (over y, core).
Axes of the slice: x: 4, y: 8, z: 8, core: 2. Of those that a mesh axis runs over, the one named last changes fastest.
Arguments:
- coeffs: float32 [4096, 128], P(('row', 'col')), may hold values from -6 to 6
- basis: float32 [256, 128, 4096], P('row', 'col'), may hold values from -0.1875 to 0.1875
- observed: float32 [256, 128, 128], P('row', 'col'), may hold values from -6 to 6
- lift_w: float32 [32], replicated, may hold values from -3 to 3
- lift_b: float32 [32], replicated, may hold values from -3 to 3
- w_one: bfloat16 [3, 3, 32, 32], replicated, may hold values from -0.375 to 0.375
- b_one: float32 [32], replicated, may hold values from -3 to 3
- w_two: bfloat16 [3, 3, 32, 32], replicated, may hold values from -0.375 to 0.375
- b_two: float32 [32], replicated, may hold values from -3 to 3
- read_w: float32 [32], replicated, may hold values from -1 to 1
Outputs:
- pressure: float32 [256, 128, 128], P('row', 'col')
- grad_coeffs: float32 [4096, 128], P(('row', 'col'))
All inputs are finite; a program needn't handle non-finite values.
Results may differ from a plain program's by a relative error of at most 0.015.
Values may be sent and summed in bfloat16 or wider, within the bound.
No kernel may reach another device: no remote copies, remote signals or barrier semaphores. Data moves between devices by JAX's collectives and lax.ppermute only.
A program may use at most 64 MiB of HBM per device.

v0:
```python
import jax
import jax.numpy as jnp
from jax import lax
from jax.sharding import PartitionSpec as P

prior_weight = 0.1


def with_halo(block, sides, width):
    for axis, dim in sides:
        count = lax.axis_size(axis)
        forward = [(i, i + 1) for i in range(count - 1)]
        backward = [(target, source) for source, target in forward]
        low = lax.ppermute(
            lax.slice_in_dim(block, block.shape[dim] - width, None, axis=dim), axis, forward
        )
        high = lax.ppermute(lax.slice_in_dim(block, 0, width, axis=dim), axis, backward)
        block = jnp.concatenate([low, block, high], axis=dim)
    return block


def extend_tile(values):
    return with_halo(values, (("row", 0), ("col", 1)), 1)


def conv_fwd(values, weights, extend):
    padded = extend(values)
    nrow = values.shape[0]
    ncol = values.shape[1]
    running = jnp.zeros(values.shape[:3] + (weights.shape[3],), jnp.float32)
    for shift_x in range(3):
        for shift_y in range(3):
            window = padded[shift_x : shift_x + nrow, shift_y : shift_y + ncol]
            running = running + jnp.einsum(
                "xybi,io->xybo",
                window,
                weights[shift_x, shift_y],
                preferred_element_type=jnp.float32,
            )
    return running


def conv_back(grads, weights, extend):
    padded = extend(grads)
    nrow = grads.shape[0]
    ncol = grads.shape[1]
    running = jnp.zeros(grads.shape[:3] + (weights.shape[2],), jnp.float32)
    for shift_x in range(3):
        for shift_y in range(3):
            window = padded[2 - shift_x : 2 - shift_x + nrow, 2 - shift_y : 2 - shift_y + ncol]
            running = running + jnp.einsum(
                "xybo,io->xybi",
                window,
                weights[shift_x, shift_y],
                preferred_element_type=jnp.float32,
            )
    return running


def surrogate(logperm, observed, lift_w, lift_b, w_one, b_one, w_two, b_two, read_w, extend):
    lifted = (logperm[..., None] * lift_w + lift_b).astype(jnp.bfloat16)
    hidden_one = jnp.tanh(conv_fwd(lifted, w_one, extend) + b_one).astype(jnp.bfloat16)
    hidden_two = jnp.tanh(conv_fwd(hidden_one, w_two, extend) + b_two)
    pressure = jnp.sum(hidden_two * read_w, axis=-1)
    misfit = pressure - observed
    grad_two = (misfit[..., None] * read_w * (1.0 - hidden_two * hidden_two)).astype(jnp.bfloat16)
    h_one = hidden_one.astype(jnp.float32)
    grad_one = (conv_back(grad_two, w_two, extend) * (1.0 - h_one * h_one)).astype(jnp.bfloat16)
    grad_field = jnp.sum(conv_back(grad_one, w_one, extend) * lift_w, axis=-1)
    return (pressure, grad_field)


def shards(coeffs, basis, observed, lift_w, lift_b, w_one, b_one, w_two, b_two, read_w):
    tile_rows, tile_cols, mode_count = basis.shape
    batch_size = coeffs.shape[1]
    flat_basis = basis.reshape(tile_rows * tile_cols, mode_count)
    basis_part = flat_basis
    logperm = jnp.dot(
        basis_part,
        lax.all_gather(coeffs, ("row", "col"), axis=0, tiled=True),
        precision=lax.Precision.HIGHEST,
        preferred_element_type=jnp.float32,
    )
    logperm = logperm.reshape(tile_rows, tile_cols, batch_size)
    pressure, grad_field = surrogate(
        logperm, observed, lift_w, lift_b, w_one, b_one, w_two, b_two, read_w, extend_tile
    )
    grad_flat = grad_field.reshape(tile_rows * tile_cols, batch_size)
    basis_part = flat_basis
    summed = lax.psum_scatter(
        lax.dot_general(
            basis_part,
            grad_flat,
            (((0,), (0,)), ((), ())),
            precision=lax.Precision.HIGHEST,
            preferred_element_type=jnp.float32,
        ),
        ("row", "col"),
        scatter_dimension=0,
        tiled=True,
    )
    grad_coeffs = summed + prior_weight * coeffs
    return (pressure, grad_coeffs)


def solution(mesh):
    return jax.shard_map(
        shards,
        mesh=mesh,
        in_specs=(
            P(("row", "col"), None),
            P("row", "col", None),
            P("row", "col", None),
            P(),
            P(),
            P(),
            P(),
            P(),
            P(),
            P(),
        ),
        out_specs=(P("row", "col", None), P(("row", "col"), None)),
        check_vma=False,
    )
```

profile of v0, /device:TPU:1, one launch (start us, length us, event | category | flops | bytes accessed | tf_op | source)
XLA Modules:
  0.0 521.0 jit_solution(12413397913941933140)
XLA Ops:
  7.2 0.7 all-gather.2.cloned.1.call-update
  8.0 126.0 %all-gather.2.cloned.1.call-done = f32[4096,128]{1,0:T(8,128)} async-done(((f32[8,128]{1,0:T(8,128)}), f32[4096,128]{1,0:T(8,128)}) %all-gather.2.cloned.1.call-update) | async-done | bytes 2097168 | tf_op jit(solution)/shard_map/all_gather | solution.py:80
  134.0 3.0 fusion
  137.2 3.0 collective-permute-start
  140.3 1.3 collective-permute-start.1
  142.0 3.3 collective-permute-done.1
  145.3 4.7 collective-permute-start.2
  150.0 1.9 collective-permute-start.3
  152.6 3.2 collective-permute-done.3
  158.3 3.1 collective-permute-start.4
  161.4 1.3 collective-permute-start.5
  163.1 3.4 collective-permute-done.5
  166.5 3.9 collective-permute-start.6
  170.4 1.9 collective-permute-start.7
  172.9 3.2 collective-permute-done.7
  178.2 0.5 multiply_reduce_fusion
  179.3 1.3 collective-permute-start.9
  180.6 4.0 collective-permute-start.8
  184.9 1.0 collective-permute-done.8
  185.9 3.0 collective-permute-start.11
  188.9 1.9 collective-permute-start.10
  191.4 3.3 collective-permute-done.10
  196.6 1.3 collective-permute-start.13
  197.9 4.7 collective-permute-start.12
  202.9 1.0 collective-permute-done.12
  204.0 2.7 collective-permute-start.15
  206.6 2.1 collective-permute-start.14
  209.3 3.1 collective-permute-done.14
  214.3 3.2 convolution_bitcast_fusion
  217.5 295.0 %all-reduce.3.cloned.1.call-done = f32[4096,128]{0,1:T(8,128)} async-done(((f32[4096,128]{0,1:T(8,128)}), f32[4096,128]{0,1:T(8,128)}) %all-reduce.3.cloned.1.call-update) | async-done | bytes 2097168
  512.5 0.9 constant_dynamic-slice_fusion
  513.5 0.6 multiply_add_fusion
  (82 shorter events, 12.9 us)
Async XLA Ops:
  7.2 126.9 %copy-start = (f32[8,8,4096]{2,1,0:T(8,128)S(1)}, f32[8,8,4096]{2,1,0:T(8,128)}, u32[]{:S(2)}) copy-start(f32[8,8,4096]{2,1,0:T(8,128)} %param.11) | copy-start | bytes 3145732
  7.2 126.8 %all-gather.2.cloned.1.call-start = ((), (), s32[]{:S(2)}) async-start(), calls=%async_computation | async-start | bytes 2101248 | tf_op jit(solution)/shard_map/all_gather | solution.py:80
  7.9 129.1 %copy-start.6 = (f32[32]{0:T(128)S(1)}, f32[32]{0:T(128)}, u32[]{:S(2)}) copy-start(f32[32]{0:T(128)} %param.13) | copy-start | bytes 388
  7.9 129.1 %copy-start.7 = (f32[32]{0:T(128)S(1)}, f32[32]{0:T(128)}, u32[]{:S(2)}) copy-start(f32[32]{0:T(128)} %param.14) | copy-start | bytes 388
  7.9 133.6 %copy-start.2 = (bf16[3,3,32,32]{3,2,1,0:T(8,128)(2,1)S(1)}, bf16[3,3,32,32]{3,2,1,0:T(8,128)(2,1)}, u32[]{:S(2)}) copy-start(bf16[3,3,32,32]{3,2,1,0:T(8,128)(2,1)} %param.15) | copy-start | bytes 55300
  7.9 504.6 %all-reduce.3.cloned.1.call-start = ((), (), s32[]{:S(2)}) async-start(), calls=%async_computation.1 | async-start | bytes 4194304
  137.2 4.7 collective-permute-start
  140.3 5.0 collective-permute-start.1
  145.3 7.2 %collective-permute-start.2 = (bf16[10,1,128,32]{2,3,1,0:T(8,128)(2,1)S(1)}, bf16[10,1,128,32]{2,3,1,0:T(8,128)(2,1)S(1)}, u32[]{:S(2)}, u32[]{:S(2)}) collective-permute-start(bf16[10,1,128,32]{2,3,1,0:T(8,128)(2,1)S(1)} %get-tuple-element.16), channel_id=1, source_target_pairs={{0,1},{1,2},{2,3},{3,4},{4,5},{5,6},{6,7},{7,8},{8,9},{9,10},{10,1... | collective-permute-start | bytes 245768 | tf_op jit(solution)/shard_map/ppermute | solution.py:14
  150.0 5.8 %collective-permute-start.3 = (bf16[10,1,128,32]{2,3,1,0:T(8,128)(2,1)S(1)}, bf16[10,1,128,32]{2,3,1,0:T(8,128)(2,1)S(1)}, u32[]{:S(2)}, u32[]{:S(2)}) collective-permute-start(bf16[10,1,128,32]{2,3,1,0:T(8,128)(2,1)S(1)} %get-tuple-element.17), channel_id=1, source_target_pairs={{1,0},{2,1},{3,2},{4,3},{5,4},{6,5},{7,6},{8,7},{9,8},{10,9},{11,1... | collective-permute-start | bytes 245768 | tf_op jit(solution)/shard_map/ppermute | solution.py:17
  157.2 0.7 copy-start.10
  157.8 4.9 copy-start.1
  158.3 4.7 collective-permute-start.4
  161.4 5.0 collective-permute-start.5
  166.5 6.5 %collective-permute-start.6 = (bf16[10,1,128,32]{2,3,1,0:T(8,128)(2,1)S(1)}, bf16[10,1,128,32]{2,3,1,0:T(8,128)(2,1)S(1)}, u32[]{:S(2)}, u32[]{:S(2)}) collective-permute-start(bf16[10,1,128,32]{2,3,1,0:T(8,128)(2,1)S(1)} %get-tuple-element.12), channel_id=1, source_target_pairs={{0,1},{1,2},{2,3},{3,4},{4,5},{5,6},{6,7},{7,8},{8,9},{9,10},{10,1... | collective-permute-start | bytes 245768 | tf_op jit(solution)/shard_map/ppermute | solution.py:14
  170.4 5.8 %collective-permute-start.7 = (bf16[10,1,128,32]{2,3,1,0:T(8,128)(2,1)S(1)}, bf16[10,1,128,32]{2,3,1,0:T(8,128)(2,1)S(1)}, u32[]{:S(2)}, u32[]{:S(2)}) collective-permute-start(bf16[10,1,128,32]{2,3,1,0:T(8,128)(2,1)S(1)} %get-tuple-element.13), channel_id=1, source_target_pairs={{1,0},{2,1},{3,2},{4,3},{5,4},{6,5},{7,6},{8,7},{9,8},{10,9},{11,1... | collective-permute-start | bytes 245768 | tf_op jit(solution)/shard_map/ppermute | solution.py:17
  177.6 0.7 copy-start.8
  177.6 0.7 copy-start.9
  178.2 0.8 copy-start.4
  178.8 6.1 %copy-start.3 = (f32[8,8,128]{2,1,0:T(8,128)}, f32[8,8,128]{2,1,0:T(8,128)S(1)}, u32[]{:S(2)}) copy-start(f32[8,8,128]{2,1,0:T(8,128)S(1)} %get-tuple-element.26) | copy-start | bytes 98308
  179.3 5.6 %collective-permute-start.9 = (bf16[1,8,128,32]{2,3,1,0:T(8,128)(2,1)S(1)}, bf16[1,8,128,32]{2,3,1,0:T(8,128)(2,1)S(1)}, u32[]{:S(2)}, u32[]{:S(2)}) collective-permute-start(bf16[1,8,128,32]{2,3,1,0:T(8,128)(2,1)S(1)} %get-tuple-element.21), channel_id=1, source_target_pairs={{16,0},{32,16},{48,32},{64,48},{80,64},{96,80},{112,96},{128,112},... | collective-permute-start | bytes 196616 | tf_op jit(solution)/shard_map/ppermute | solution.py:17
  180.6 5.3 %collective-permute-start.8 = (bf16[1,8,128,32]{2,3,1,0:T(8,128)(2,1)S(1)}, bf16[1,8,128,32]{2,3,1,0:T(8,128)(2,1)S(1)}, u32[]{:S(2)}, u32[]{:S(2)}) collective-permute-start(bf16[1,8,128,32]{2,3,1,0:T(8,128)(2,1)S(1)} %get-tuple-element.20), channel_id=1, source_target_pairs={{0,16},{16,32},{32,48},{48,64},{64,80},{80,96},{96,112},{112,128},... | collective-permute-start | bytes 196616 | tf_op jit(solution)/shard_map/ppermute | solution.py:14
  185.9 9.3 %collective-permute-start.11 = (bf16[10,1,128,32]{2,3,1,0:T(8,128)(2,1)S(1)}, bf16[10,1,128,32]{2,3,1,0:T(8,128)(2,1)S(1)}, u32[]{:S(2)}, u32[]{:S(2)}) collective-permute-start(bf16[10,1,128,32]{2,3,1,0:T(8,128)(2,1)S(1)} %get-tuple-element.9), channel_id=1, source_target_pairs={{0,1},{1,2},{2,3},{3,4},{4,5},{5,6},{6,7},{7,8},{8,9},{9,10},{10,1... | collective-permute-start | bytes 245768 | tf_op jit(solution)/shard_map/ppermute | solution.py:14
  188.9 5.8 %collective-permute-start.10 = (bf16[10,1,128,32]{2,3,1,0:T(8,128)(2,1)S(1)}, bf16[10,1,128,32]{2,3,1,0:T(8,128)(2,1)S(1)}, u32[]{:S(2)}, u32[]{:S(2)}) collective-permute-start(bf16[10,1,128,32]{2,3,1,0:T(8,128)(2,1)S(1)} %get-tuple-element.8), channel_id=1, source_target_pairs={{1,0},{2,1},{3,2},{4,3},{5,4},{6,5},{7,6},{8,7},{9,8},{10,9},{11,1... | collective-permute-start | bytes 245768 | tf_op jit(solution)/shard_map/ppermute | solution.py:17
  196.6 6.3 %collective-permute-start.13 = (bf16[1,8,128,32]{2,3,1,0:T(8,128)(2,1)S(1)}, bf16[1,8,128,32]{2,3,1,0:T(8,128)(2,1)S(1)}, u32[]{:S(2)}, u32[]{:S(2)}) collective-permute-start(bf16[1,8,128,32]{2,3,1,0:T(8,128)(2,1)S(1)} %get-tuple-element.19), channel_id=1, source_target_pairs={{16,0},{32,16},{48,32},{64,48},{80,64},{96,80},{112,96},{128,112},... | collective-permute-start | bytes 196616 | tf_op jit(solution)/shard_map/ppermute | solution.py:17
  197.9 6.0 %collective-permute-start.12 = (bf16[1,8,128,32]{2,3,1,0:T(8,128)(2,1)S(1)}, bf16[1,8,128,32]{2,3,1,0:T(8,128)(2,1)S(1)}, u32[]{:S(2)}, u32[]{:S(2)}) collective-permute-start(bf16[1,8,128,32]{2,3,1,0:T(8,128)(2,1)S(1)} %get-tuple-element.18), channel_id=1, source_target_pairs={{0,16},{16,32},{32,48},{48,64},{64,80},{80,96},{96,112},{112,128},... | collective-permute-start | bytes 196616 | tf_op jit(solution)/shard_map/ppermute | solution.py:14
  204.0 9.0 %collective-permute-start.15 = (bf16[10,1,128,32]{2,3,1,0:T(8,128)(2,1)S(1)}, bf16[10,1,128,32]{2,3,1,0:T(8,128)(2,1)S(1)}, u32[]{:S(2)}, u32[]{:S(2)}) collective-permute-start(bf16[10,1,128,32]{2,3,1,0:T(8,128)(2,1)S(1)} %get-tuple-element.7), channel_id=1, source_target_pairs={{0,1},{1,2},{2,3},{3,4},{4,5},{5,6},{6,7},{7,8},{8,9},{9,10},{10,1... | collective-permute-start | bytes 245768 | tf_op jit(solution)/shard_map/ppermute | solution.py:14
  206.6 5.8 %collective-permute-start.14 = (bf16[10,1,128,32]{2,3,1,0:T(8,128)(2,1)S(1)}, bf16[10,1,128,32]{2,3,1,0:T(8,128)(2,1)S(1)}, u32[]{:S(2)}, u32[]{:S(2)}) collective-permute-start(bf16[10,1,128,32]{2,3,1,0:T(8,128)(2,1)S(1)} %get-tuple-element.6), channel_id=1, source_target_pairs={{1,0},{2,1},{3,2},{4,3},{5,4},{6,5},{7,6},{8,7},{9,8},{10,9},{11,1... | collective-permute-start | bytes 245768 | tf_op jit(solution)/shard_map/ppermute | solution.py:17
  217.5 296.0 %copy-start.5 = (f32[8,128]{1,0:T(8,128)S(1)}, f32[8,128]{1,0:T(8,128)}, u32[]{:S(2)}) copy-start(f32[8,128]{1,0:T(8,128)} %param.10) | copy-start | bytes 12292
Sparse Core Ops, SparseCore 0:
  12.2 121.8 all-gather.1
  217.6 294.8 all-reduce.2
where the time goes:
time: 522 us; the launch traced here: 521 us
  waiting for transfers between devices  443 us (85%)
  starting transfers between devices  42.1 us (8%)
  matrix products  18 us (3%)
  between operations  14.6 us (3%)
    unnamed x3, waiting for transfers between devices  296 us
    all_gather x1, waiting for transfers between devices, shards(): lax.all_gather(coeffs, ('row', 'col'), axis=0, tiled=True)  126 us
    ppermute x8, starting transfers between devices, with_halo(): lax.ppermute(lax.slice_in_dim(block, block.shape[dim] - width, None, axis...  29 us
    ppermute x8, waiting for transfers between devices, with_halo(): lax.ppermute(lax.slice_in_dim(block, 0, width, axis=dim), axis, backward)  19.4 us
    ppermute x8, starting transfers between devices, with_halo(): lax.ppermute(lax.slice_in_dim(block, 0, width, axis=dim), axis, backward)  13 us
  transfers between devices with their start and end apart: 18, of which 10 were waited for; matrix products, arithmetic and copies ran while one was open for 1% of the time, Pallas kernels for 0%

commit v1 on v0

--- a/solution.py
+++ b/solution.py
@@ -77,7 +77,12 @@
     basis_part = flat_basis
     logperm = jnp.dot(
         basis_part,
-        lax.all_gather(coeffs, ("row", "col"), axis=0, tiled=True),
+        jnp.concatenate(
+            lax.all_to_all(
+                jnp.stack([coeffs] * lax.axis_size(("row", "col"))), ("row", "col"), 0, 0
+            ),
+            axis=0,
+        ),
         precision=lax.Precision.HIGHEST,
         preferred_element_type=jnp.float32,
     )

time: 522 us -> 469 us (0.90)
  waiting for transfers between devices: 443 us -> 316 us
  blocking collectives: 0 us -> 77 us
    all_gather x1 -> x0, waiting for transfers between devices: 126 us -> none  [shards(): lax.all_gather(coeffs, ('row', 'col'), axis=0, tiled=True)]
    all_to_all x0 -> x1, blocking collectives: none -> 77 us  [shards(): lax.all_to_all(jnp.stack([coeffs] * lax.axis_size(('row', 'col'))), ('row...]
    unnamed x3 -> x2, waiting for transfers between devices: 296 us -> 294 us
  transfers between devices with their start and end apart: 18 -> 17, of which waited for: 10 -> 9; matrix products, arithmetic and copies ran while one was open for 1% -> 1% of each run, Pallas kernels for 0% -> 0%
where the time goes in v1:
time: 469 us; the launch traced here: 468 us
  waiting for transfers between devices  316 us (67%)
  blocking collectives  77 us (16%)
  starting transfers between devices  40.6 us (9%)
  matrix products  16.3 us (3%)
  between operations  14.6 us (3%)
    unnamed x2, waiting for transfers between devices  294 us
    all_to_all x1, blocking collectives, shards(): lax.all_to_all(jnp.stack([coeffs] * lax.axis_size(('row', 'col'))), ('row...  77 us
    ppermute x8, starting transfers between devices, with_halo(): lax.ppermute(lax.slice_in_dim(block, block.shape[dim] - width, None, axis...  27.5 us
    ppermute x8, waiting for transfers between devices, with_halo(): lax.ppermute(lax.slice_in_dim(block, 0, width, axis=dim), axis, backward)  19.4 us
    ppermute x8, starting transfers between devices, with_halo(): lax.ppermute(lax.slice_in_dim(block, 0, width, axis=dim), axis, backward)  13 us
  transfers between devices with their start and end apart: 17, of which 9 were waited for; matrix products, arithmetic and copies ran while one was open for 1% of the time, Pallas kernels for 0%

profile of v1, /device:TPU:1, one launch (start us, length us, event | category | flops | bytes accessed | tf_op | source)
XLA Modules:
  0.0 468.3 jit_solution(9981590018778538026)
XLA Ops:
  7.2 0.9 stack.2
  8.1 77.0 %all_to_all.5 = f32[512,8,128]{2,1,0:T(8,128)S(1)} all-to-all(f32[512,8,128]{2,1,0:T(8,128)S(1)} %stack.2), channel_id=1, replica_groups=mesh['row'=32,'col'=16] {'row','col'}, dimensions={0} | all-to-all | bytes 4194304 | tf_op jit(solution)/shard_map/all_to_all | solution.py:81
  85.1 1.4 fusion
  86.8 2.6 collective-permute-start
  89.4 1.3 collective-permute-start.1
  91.1 3.3 collective-permute-done.1
  94.4 4.4 collective-permute-start.2
  98.8 1.9 collective-permute-start.3
  101.4 3.2 collective-permute-done.3
  107.1 2.3 collective-permute-start.4
  109.5 1.3 collective-permute-start.5
  111.1 3.4 collective-permute-done.5
  114.5 4.0 collective-permute-start.6
  118.5 1.9 collective-permute-start.7
  121.0 3.2 collective-permute-done.7
  126.3 0.5 multiply_reduce_fusion
  127.4 1.3 collective-permute-start.9
  128.7 4.1 collective-permute-start.8
  133.0 1.0 collective-permute-done.8
  134.1 2.9 collective-permute-start.11
  137.0 2.1 collective-permute-start.10
  139.7 3.1 collective-permute-done.10
  144.7 1.3 collective-permute-start.13
  146.0 4.6 collective-permute-start.12
  151.0 1.0 collective-permute-done.12
  152.0 2.7 collective-permute-start.15
  154.7 1.9 collective-permute-start.14
  157.2 3.3 collective-permute-done.14
  162.4 3.2 convolution_bitcast_fusion
  165.6 294.3 %all-reduce.3.cloned.1.call-done = f32[4096,128]{0,1:T(8,128)} async-done(((f32[4096,128]{0,1:T(8,128)}), f32[4096,128]{0,1:T(8,128)}) %all-reduce.3.cloned.1.call-update) | async-done | bytes 2097168
  459.9 0.9 constant_dynamic-slice_fusion
  460.9 0.6 multiply_add_fusion
  (81 shorter events, 12.9 us)
Async XLA Ops:
  7.2 78.0 %copy-start = (f32[8,8,4096]{2,1,0:T(8,128)S(1)}, f32[8,8,4096]{2,1,0:T(8,128)}, u32[]{:S(2)}) copy-start(f32[8,8,4096]{2,1,0:T(8,128)} %param.11) | copy-start | bytes 3145732
  7.2 452.7 %all-reduce.3.cloned.1.call-start = ((), (), s32[]{:S(2)}) async-start(), calls=%async_computation.1 | async-start | bytes 4194304
  85.1 1.4 copy-start.6
  85.1 1.4 copy-start.7
  85.1 5.5 %copy-start.2 = (bf16[3,3,32,32]{3,2,1,0:T(8,128)(2,1)S(1)}, bf16[3,3,32,32]{3,2,1,0:T(8,128)(2,1)}, u32[]{:S(2)}) copy-start(bf16[3,3,32,32]{3,2,1,0:T(8,128)(2,1)} %param.15) | copy-start | bytes 55300
  86.8 4.3 collective-permute-start
  89.4 5.0 %collective-permute-start.1 = (bf16[1,8,128,32]{2,3,1,0:T(8,128)(2,1)S(1)}, bf16[1,8,128,32]{2,3,1,0:T(8,128)(2,1)S(1)}, u32[]{:S(2)}, u32[]{:S(2)}) collective-permute-start(bf16[1,8,128,32]{2,3,1,0:T(8,128)(2,1)S(1)} %get-tuple-element.25), channel_id=1, source_target_pairs={{16,0},{32,16},{48,32},{64,48},{80,64},{96,80},{112,96},{128,112},... | collective-permute-start | bytes 196616 | tf_op jit(solution)/shard_map/ppermute | solution.py:17
  94.4 7.0 %collective-permute-start.2 = (bf16[10,1,128,32]{2,3,1,0:T(8,128)(2,1)S(1)}, bf16[10,1,128,32]{2,3,1,0:T(8,128)(2,1)S(1)}, u32[]{:S(2)}, u32[]{:S(2)}) collective-permute-start(bf16[10,1,128,32]{2,3,1,0:T(8,128)(2,1)S(1)} %get-tuple-element.16), channel_id=1, source_target_pairs={{0,1},{1,2},{2,3},{3,4},{4,5},{5,6},{6,7},{7,8},{8,9},{9,10},{10,1... | collective-permute-start | bytes 245768 | tf_op jit(solution)/shard_map/ppermute | solution.py:14
  98.8 5.8 %collective-permute-start.3 = (bf16[10,1,128,32]{2,3,1,0:T(8,128)(2,1)S(1)}, bf16[10,1,128,32]{2,3,1,0:T(8,128)(2,1)S(1)}, u32[]{:S(2)}, u32[]{:S(2)}) collective-permute-start(bf16[10,1,128,32]{2,3,1,0:T(8,128)(2,1)S(1)} %get-tuple-element.17), channel_id=1, source_target_pairs={{1,0},{2,1},{3,2},{4,3},{5,4},{6,5},{7,6},{8,7},{9,8},{10,9},{11,1... | collective-permute-start | bytes 245768 | tf_op jit(solution)/shard_map/ppermute | solution.py:17
  106.0 0.7 copy-start.10
  106.6 4.1 copy-start.1
  107.1 4.0 collective-permute-start.4
  109.5 5.0 %collective-permute-start.5 = (bf16[1,8,128,32]{2,3,1,0:T(8,128)(2,1)S(1)}, bf16[1,8,128,32]{2,3,1,0:T(8,128)(2,1)S(1)}, u32[]{:S(2)}, u32[]{:S(2)}) collective-permute-start(bf16[1,8,128,32]{2,3,1,0:T(8,128)(2,1)S(1)} %get-tuple-element.23), channel_id=1, source_target_pairs={{16,0},{32,16},{48,32},{64,48},{80,64},{96,80},{112,96},{128,112},... | collective-permute-start | bytes 196616 | tf_op jit(solution)/shard_map/ppermute | solution.py:17
  114.5 6.5 %collective-permute-start.6 = (bf16[10,1,128,32]{2,3,1,0:T(8,128)(2,1)S(1)}, bf16[10,1,128,32]{2,3,1,0:T(8,128)(2,1)S(1)}, u32[]{:S(2)}, u32[]{:S(2)}) collective-permute-start(bf16[10,1,128,32]{2,3,1,0:T(8,128)(2,1)S(1)} %get-tuple-element.12), channel_id=1, source_target_pairs={{0,1},{1,2},{2,3},{3,4},{4,5},{5,6},{6,7},{7,8},{8,9},{9,10},{10,1... | collective-permute-start | bytes 245768 | tf_op jit(solution)/shard_map/ppermute | solution.py:14
  118.5 5.8 %collective-permute-start.7 = (bf16[10,1,128,32]{2,3,1,0:T(8,128)(2,1)S(1)}, bf16[10,1,128,32]{2,3,1,0:T(8,128)(2,1)S(1)}, u32[]{:S(2)}, u32[]{:S(2)}) collective-permute-start(bf16[10,1,128,32]{2,3,1,0:T(8,128)(2,1)S(1)} %get-tuple-element.13), channel_id=1, source_target_pairs={{1,0},{2,1},{3,2},{4,3},{5,4},{6,5},{7,6},{8,7},{9,8},{10,9},{11,1... | collective-permute-start | bytes 245768 | tf_op jit(solution)/shard_map/ppermute | solution.py:17
  125.6 0.7 copy-start.8
  125.7 0.7 copy-start.9
  126.3 0.8 copy-start.4
  126.9 6.1 %copy-start.3 = (f32[8,8,128]{2,1,0:T(8,128)}, f32[8,8,128]{2,1,0:T(8,128)S(1)}, u32[]{:S(2)}) copy-start(f32[8,8,128]{2,1,0:T(8,128)S(1)} %get-tuple-element.26) | copy-start | bytes 98308
  127.4 5.7 %collective-permute-start.9 = (bf16[1,8,128,32]{2,3,1,0:T(8,128)(2,1)S(1)}, bf16[1,8,128,32]{2,3,1,0:T(8,128)(2,1)S(1)}, u32[]{:S(2)}, u32[]{:S(2)}) collective-permute-start(bf16[1,8,128,32]{2,3,1,0:T(8,128)(2,1)S(1)} %get-tuple-element.21), channel_id=1, source_target_pairs={{16,0},{32,16},{48,32},{64,48},{80,64},{96,80},{112,96},{128,112},... | collective-permute-start | bytes 196616 | tf_op jit(solution)/shard_map/ppermute | solution.py:17
  128.7 5.4 %collective-permute-start.8 = (bf16[1,8,128,32]{2,3,1,0:T(8,128)(2,1)S(1)}, bf16[1,8,128,32]{2,3,1,0:T(8,128)(2,1)S(1)}, u32[]{:S(2)}, u32[]{:S(2)}) collective-permute-start(bf16[1,8,128,32]{2,3,1,0:T(8,128)(2,1)S(1)} %get-tuple-element.20), channel_id=1, source_target_pairs={{0,16},{16,32},{32,48},{48,64},{64,80},{80,96},{96,112},{112,128},... | collective-permute-start | bytes 196616 | tf_op jit(solution)/shard_map/ppermute | solution.py:14
  134.1 9.3 %collective-permute-start.11 = (bf16[10,1,128,32]{2,3,1,0:T(8,128)(2,1)S(1)}, bf16[10,1,128,32]{2,3,1,0:T(8,128)(2,1)S(1)}, u32[]{:S(2)}, u32[]{:S(2)}) collective-permute-start(bf16[10,1,128,32]{2,3,1,0:T(8,128)(2,1)S(1)} %get-tuple-element.9), channel_id=1, source_target_pairs={{0,1},{1,2},{2,3},{3,4},{4,5},{5,6},{6,7},{7,8},{8,9},{9,10},{10,1... | collective-permute-start | bytes 245768 | tf_op jit(solution)/shard_map/ppermute | solution.py:14
  137.0 5.8 %collective-permute-start.10 = (bf16[10,1,128,32]{2,3,1,0:T(8,128)(2,1)S(1)}, bf16[10,1,128,32]{2,3,1,0:T(8,128)(2,1)S(1)}, u32[]{:S(2)}, u32[]{:S(2)}) collective-permute-start(bf16[10,1,128,32]{2,3,1,0:T(8,128)(2,1)S(1)} %get-tuple-element.8), channel_id=1, source_target_pairs={{1,0},{2,1},{3,2},{4,3},{5,4},{6,5},{7,6},{8,7},{9,8},{10,9},{11,1... | collective-permute-start | bytes 245768 | tf_op jit(solution)/shard_map/ppermute | solution.py:17
  144.7 6.2 %collective-permute-start.13 = (bf16[1,8,128,32]{2,3,1,0:T(8,128)(2,1)S(1)}, bf16[1,8,128,32]{2,3,1,0:T(8,128)(2,1)S(1)}, u32[]{:S(2)}, u32[]{:S(2)}) collective-permute-start(bf16[1,8,128,32]{2,3,1,0:T(8,128)(2,1)S(1)} %get-tuple-element.19), channel_id=1, source_target_pairs={{16,0},{32,16},{48,32},{64,48},{80,64},{96,80},{112,96},{128,112},... | collective-permute-start | bytes 196616 | tf_op jit(solution)/shard_map/ppermute | solution.py:17
  146.0 6.0 %collective-permute-start.12 = (bf16[1,8,128,32]{2,3,1,0:T(8,128)(2,1)S(1)}, bf16[1,8,128,32]{2,3,1,0:T(8,128)(2,1)S(1)}, u32[]{:S(2)}, u32[]{:S(2)}) collective-permute-start(bf16[1,8,128,32]{2,3,1,0:T(8,128)(2,1)S(1)} %get-tuple-element.18), channel_id=1, source_target_pairs={{0,16},{16,32},{32,48},{48,64},{64,80},{80,96},{96,112},{112,128},... | collective-permute-start | bytes 196616 | tf_op jit(solution)/shard_map/ppermute | solution.py:14
  152.0 9.0 %collective-permute-start.15 = (bf16[10,1,128,32]{2,3,1,0:T(8,128)(2,1)S(1)}, bf16[10,1,128,32]{2,3,1,0:T(8,128)(2,1)S(1)}, u32[]{:S(2)}, u32[]{:S(2)}) collective-permute-start(bf16[10,1,128,32]{2,3,1,0:T(8,128)(2,1)S(1)} %get-tuple-element.7), channel_id=1, source_target_pairs={{0,1},{1,2},{2,3},{3,4},{4,5},{5,6},{6,7},{7,8},{8,9},{9,10},{10,1... | collective-permute-start | bytes 245768 | tf_op jit(solution)/shard_map/ppermute | solution.py:14
  154.7 5.8 %collective-permute-start.14 = (bf16[10,1,128,32]{2,3,1,0:T(8,128)(2,1)S(1)}, bf16[10,1,128,32]{2,3,1,0:T(8,128)(2,1)S(1)}, u32[]{:S(2)}, u32[]{:S(2)}) collective-permute-start(bf16[10,1,128,32]{2,3,1,0:T(8,128)(2,1)S(1)} %get-tuple-element.6), channel_id=1, source_target_pairs={{1,0},{2,1},{3,2},{4,3},{5,4},{6,5},{7,6},{8,7},{9,8},{10,9},{11,1... | collective-permute-start | bytes 245768 | tf_op jit(solution)/shard_map/ppermute | solution.py:17
  165.5 295.3 %copy-start.5 = (f32[8,128]{1,0:T(8,128)S(1)}, f32[8,128]{1,0:T(8,128)}, u32[]{:S(2)}) copy-start(f32[8,128]{1,0:T(8,128)} %param.10) | copy-start | bytes 12292
Sparse Core Ops, SparseCore 0:
  165.7 294.1 all-reduce.2
